TPU v7x, 32 devices: a whole 2x2x4 slice. The times are simulated.
32 devices in a mesh: seq: 8 (over y, x, core), head: 4 (over z).
Axes of the slice: x: 2, y: 2, z: 4, core: 2. Of those that a mesh axis runs over, the one named last changes fastest.
Arguments:
- tokens: bfloat16 [4096, 5376], P('seq', 'head'), may hold values from -32 to 32
- query_weight: bfloat16 [5376, 4096], P(None, 'head'), may hold values from -1 to 1
- key_weight: bfloat16 [5376, 2048], P(None, 'head'), may hold values from -1 to 1
- value_weight: bfloat16 [5376, 2048], P(None, 'head'), may hold values from -0.078125 to 0.078125
- output_grad: bfloat16 [4096, 4096], P('seq', 'head'), may hold values from -48 to 48
- segments: int32 [4096], replicated, may hold values from 0 to 3, never falling along the last dimension, each value on 1 to 2048 neighbouring positions
Outputs:
- token_grad: bfloat16 [4096, 5376], P('seq', 'head')
- query_weight_grad: bfloat16 [5376, 4096], P('seq', 'head')
- key_weight_grad: bfloat16 [5376, 2048], P('seq', 'head')
- value_weight_grad: bfloat16 [5376, 2048], P('seq', 'head')
Inputs may be any that keep to these rules, and one draw needn't show every extreme that they name: `segments`: segment numbers never fall along the tokens; a segment has at most 2048 tokens.
All inputs are finite; a program needn't handle non-finite values.
Results may differ from a plain program's by a relative error of at most 0.015.
The roundings to bfloat16 on the way count: a program that leaves them out, or rounds other values in their place, can miss the bound.
Values may be sent and summed in bfloat16 or wider, within the bound.
No kernel may reach another device: no remote copies, remote signals or barrier semaphores. Data moves between devices by JAX's collectives and lax.ppermute only.
A program may use at most 192 MiB of HBM per device.

v0:
```python
import jax
import jax.numpy as jnp
from jax import lax
from jax.sharding import PartitionSpec as P

D = 5376
HEADS = 32
KV_HEADS = 16
HEAD_DIM = 128
WINDOW = 1024
HOPS = 2
neg_large = -1e30


def passed_along(x, axis, by):
    count = lax.axis_size(axis)
    pairs = [(i, i + by) for i in range(count) if 0 <= i + by < count]
    return lax.ppermute(x, axis, pairs)


def contract_last(left, right):
    return lax.dot_general(
        left, right, (((1,), (1,)), ((), ())), preferred_element_type=jnp.float32
    )


def contract_first(left, right):
    return lax.dot_general(
        left, right, (((0,), (0,)), ((), ())), preferred_element_type=jnp.float32
    )


def attend(queries, key_value, grads, query_first, key_first, seg_query, seg_key):
    tok_rows = queries.shape[0]
    key_rows = key_value.shape[1]
    groups = HEADS // KV_HEADS
    kv_local = key_value.shape[2] // HEAD_DIM
    score_scale = (D / HEADS) ** (-0.5)
    query_four = queries.reshape(tok_rows, kv_local, groups, HEAD_DIM)
    grad_four = grads.reshape(tok_rows, kv_local, groups, HEAD_DIM)
    key_three = key_value[0].reshape(key_rows, kv_local, HEAD_DIM)
    value_three = key_value[1].reshape(key_rows, kv_local, HEAD_DIM)
    query_pos = query_first + jnp.arange(tok_rows, dtype=jnp.int32)
    key_pos = key_first + jnp.arange(key_rows, dtype=jnp.int32)
    spacing = query_pos[:, None] - key_pos[None, :]
    allowed = (
        (key_pos >= 0)[None, :]
        & (spacing >= 0)
        & (spacing < WINDOW)
        & (seg_query[:, None] == seg_key[None, :])
    )
    scores = (
        jnp.einsum("akgd,ckd->kgac", query_four, key_three, preferred_element_type=jnp.float32)
        * score_scale
    )
    masked = jnp.where(allowed, scores, neg_large)
    row_max = jnp.max(masked, axis=-1, keepdims=True)
    expo = jnp.where(allowed, jnp.exp(masked - row_max), 0.0)
    probs = expo / jnp.sum(expo, axis=-1, keepdims=True)
    dprobs = jnp.einsum(
        "akgd,ckd->kgac", grad_four, value_three, preferred_element_type=jnp.float32
    )
    center = jnp.sum(probs * dprobs, axis=-1, keepdims=True)
    dscores = (probs * (dprobs - center)).astype(jnp.bfloat16)
    probs_low = probs.astype(jnp.bfloat16)
    query_grad = (
        (
            jnp.einsum("kgac,ckd->akgd", dscores, key_three, preferred_element_type=jnp.float32)
            * score_scale
        )
        .reshape(tok_rows, -1)
        .astype(jnp.bfloat16)
    )
    key_grad = (
        jnp.einsum("kgac,akgd->ckd", dscores, query_four, preferred_element_type=jnp.float32)
        * score_scale
    ).reshape(key_rows, -1)
    value_grad = jnp.einsum(
        "kgac,akgd->ckd", probs_low, grad_four, preferred_element_type=jnp.float32
    ).reshape(key_rows, -1)
    return (query_grad, jnp.stack([key_grad, value_grad]))


def per_device(tokens, query_weight, key_weight, value_weight, output_grad, segments):
    tok_rows = tokens.shape[0]
    hop_count = HOPS
    margin = hop_count * tok_rows
    gathered = lax.all_gather(tokens, "head", axis=1, tiled=True)
    queries = jnp.dot(gathered, query_weight, preferred_element_type=jnp.float32).astype(
        jnp.bfloat16
    )
    keys_own = jnp.dot(gathered, key_weight, preferred_element_type=jnp.float32).astype(
        jnp.bfloat16
    )
    values_own = jnp.dot(gathered, value_weight, preferred_element_type=jnp.float32).astype(
        jnp.bfloat16
    )
    key_value = jnp.stack([keys_own, values_own])
    blocks = [key_value] * (hop_count + 1)
    moving = key_value
    for distance in range(1, hop_count + 1):
        moving = passed_along(moving, "seq", 1)
        blocks[hop_count - distance] = moving
    keys_all = jnp.concatenate(blocks, axis=1)
    position = lax.axis_index("seq")
    query_first = position * tok_rows
    seg_query = lax.dynamic_slice_in_dim(segments, query_first, tok_rows, 0)
    seg_padded = jnp.concatenate([jnp.full((margin,), -1, jnp.int32), segments], axis=0)
    seg_key = lax.dynamic_slice_in_dim(seg_padded, query_first, (hop_count + 1) * tok_rows, 0)
    query_grad, kv_grad = attend(
        queries, keys_all, output_grad, query_first, query_first - margin, seg_query, seg_key
    )
    pieces = [
        kv_grad[:, block * tok_rows : (block + 1) * tok_rows] for block in range(hop_count + 1)
    ]
    carried = pieces[0]
    for distance in range(1, hop_count + 1):
        carried = pieces[distance] + passed_along(carried.astype(jnp.bfloat16), "seq", -1).astype(
            carried.dtype
        )
    key_grad = carried[0].astype(jnp.bfloat16)
    value_grad = carried[1].astype(jnp.bfloat16)
    partial_term = (
        contract_last(query_grad, query_weight)
        + contract_last(key_grad, key_weight)
        + contract_last(value_grad, value_weight)
    )
    token_grad = lax.psum_scatter(
        partial_term.astype(jnp.bfloat16), "head", scatter_dimension=1, tiled=True
    )
    proj_grads = jnp.concatenate([query_grad, key_grad, value_grad], axis=1)
    summed = lax.psum_scatter(
        contract_first(gathered, proj_grads).astype(jnp.bfloat16),
        "seq",
        scatter_dimension=0,
        tiled=True,
    ).astype(jnp.float32)
    summed = summed * (tok_rows * lax.axis_size("seq")) ** (-0.5)
    q_width = query_weight.shape[1]
    k_width = key_weight.shape[1]
    query_weight_grad = summed[:, :q_width].astype(jnp.bfloat16)
    key_weight_grad = summed[:, q_width : q_width + k_width].astype(jnp.bfloat16)
    value_weight_grad = summed[:, q_width + k_width :].astype(jnp.bfloat16)
    return (token_grad, query_weight_grad, key_weight_grad, value_weight_grad)


def solution(mesh):
    in_specs = (
        P("seq", "head"),
        P(None, "head"),
        P(None, "head"),
        P(None, "head"),
        P("seq", "head"),
        P(),
    )
    out_specs = (P("seq", "head"), P("seq", "head"), P("seq", "head"), P("seq", "head"))
    return jax.shard_map(
        per_device, mesh=mesh, in_specs=in_specs, out_specs=out_specs, check_vma=False
    )
```

profile of v0, /device:TPU:0, one launch (start us, length us, event | category | flops | bytes accessed | tf_op | source)
XLA Modules:
  0.0 569.0 jit_solution(12160398720478876539)
XLA Ops:
  7.9 106.7 %all-gather.2.cloned.1.call-done = bf16[512,5376]{0,1:T(8,128)(2,1)} async-done(((bf16[512,1344]{0,1:T(8,128)(2,1)}), bf16[512,5376]{0,1:T(8,128)(2,1)}) %all-gather.2.cloned.1.call-update) | async-done | bytes 5505040 | tf_op jit(solution)/shard_map/all_gather | solution.py:88
  114.7 7.3 %fusion.32 = bf16[1,512,512]{2,1,0:T(8,128)(2,1)S(1)} fusion(bf16[512,5376]{0,1:T(8,128)(2,1)} %all-gather.2.cloned.1.call-done, bf16[5376,512]{1,0:T(8,128)(2,1)} %param.9), kind=kOutput, calls=%fused_computation.52 | convolution fusion | flops 2818834432 | bytes 11534336 | tf_op jit(solution)/shard_map/dot_general | solution.py:95
  122.1 5.7 fusion.31
  127.9 2.9 collective-permute-start
  134.9 10.3 %collective-permute-start.1 = (bf16[2,512,512]{2,1,0:T(8,128)(2,1)}, bf16[2,512,512]{2,1,0:T(8,128)(2,1)S(1)}, u32[]{:S(2)}, u32[]{:S(2)}) collective-permute-start(bf16[2,512,512]{2,1,0:T(8,128)(2,1)} %collective-permute-done), channel_id=1, source_target_pairs={{0,4},{4,8},{8,12},{12,16},{16,20},{20,24},{24,28},{1,5},{5,9},{9,... | collective-permute-start | bytes 3145736 | tf_op jit(solution)/shard_map/ppermute | solution.py:18
  145.2 10.4 %convolution_convert_fusion.1 = bf16[512,1024]{1,0:T(8,128)(2,1)S(1)} fusion(bf16[512,5376]{0,1:T(8,128)(2,1)} %all-gather.2.cloned.1.call-done, bf16[5376,1024]{1,0:T(8,128)(2,1)} %param.7), kind=kOutput, calls=%fused_computation.48 | convolution fusion | flops 5637668864 | bytes 17563648 | tf_op jit(solution)/shard_map/dot_general | solution.py:89
  161.1 2.8 reshape_squeeze.7
  163.9 17.4 %fusion.39 = (f32[4,2,512]{2,1,0:T(2,128)S(1)}, f32[4,2,512,1536]{2,3,1,0:T(8,128)}) fusion(pred[512,1536]{0,1:T(8,128)(4,1)} %fusion.16, bf16[1536,4,128,1]{0,2,3,1:T(8,128)(2,1)S(1)} %copy.38, bf16[512,4,2,128]{0,3,2,1:T(8,128)(2,1)} %bitcast.77), kind=kOutput, calls=%fused_computation.66 | convolution fusion | flops 1642071552 | bytes 28590080 | tf_op jit(solution)/shard_map/sub | solution.py:58
  181.3 12.5 %fusion.6 = f32[4,1536,128,1]{1,2,3,0:T(8,128)} fusion(bf16[512,4,2,128]{0,3,2,1:T(8,128)(2,1)} %bitcast.80, f32[4,2,512,1536]{2,3,1,0:T(8,128)} %get-tuple-element.19, f32[4,2,512]{2,1,0:T(2,128)S(1)} %get-tuple-element.18), kind=kOutput, calls=%fused_computation.11 | convolution fusion | flops 1623195648 | bytes 29376512 | tf_op jit(solution)/shard_map/kgac,akgd->ckd/dot_general | solution.py:78
  193.8 16.6 %fusion.1 = (f32[4,2,512]{2,1,0:T(2,128)S(1)}, f32[4,1536,512,2]{2,1,3,0:T(8,128)}) fusion(f32[4,2,512,1536]{2,3,1,0:T(8,128)} %get-tuple-element.19, f32[4,2,512]{2,1,0:T(2,128)S(1)} %get-tuple-element.18, bf16[512,4,2,128]{0,3,2,1:T(8,128)(2,1)S(1)} %bitcast.81, bf16[1536,4,128,1]{2,1,0,3:T(4,128)(2,1)S(1)} %bitcast.79), kind=kOutput, calls=%fused_computation.3 | convolution fusion | flops 1629483008 | bytes 52985856 | tf_op jit(solution)/shard_map/akgd,ckd->kgac/dot_general | solution.py:60
  210.4 16.8 %fusion.3 = bf16[4,2,512,1536]{2,3,1,0:T(8,128)(2,1)S(1)} fusion(f32[4,1536,512,2]{2,1,3,0:T(8,128)} %get-tuple-element.21, f32[4,2,512]{2,1,0:T(2,128)S(1)} %get-tuple-element.20, f32[4,2,512,1536]{2,3,1,0:T(8,128)} %get-tuple-element.19, f32[4,2,512]{2,1,0:T(2,128)S(1)} %get-tuple-element.18), kind=kLoop, calls=%fused_computation.5 | loop fusion | flops 25165824 | bytes 62947328 | tf_op jit(solution)/shard_map/convert_element_type | solution.py:64
  227.2 7.0 %fusion.13 = f32[4,128,1536]{2,1,0:T(8,128)} fusion(bf16[512,4,2,128]{0,3,2,1:T(8,128)(2,1)} %bitcast.78, bf16[4,2,512,1536]{2,3,1,0:T(8,128)(2,1)S(1)} %fusion.3), kind=kOutput, calls=%fused_computation.27 | convolution fusion | flops 1611399168 | bytes 16777216 | tf_op jit(solution)/shard_map/kgac,akgd->ckd/dot_general | solution.py:75
  237.7 5.4 collective-permute-done.2
  244.8 2.8 multiply_convert_fusion.1
  247.6 12.7 %collective-permute-done.3 = bf16[2,512,512]{1,2,0:T(8,128)(2,1)S(1)} collective-permute-done((bf16[2,512,512]{1,2,0:T(8,128)(2,1)S(1)}, bf16[2,512,512]{1,2,0:T(8,128)(2,1)S(1)}, u32[]{:S(2)}, u32[]{:S(2)}) %collective-permute-start.3) | collective-permute-done | bytes 1048608 | tf_op jit(solution)/shard_map/ppermute | solution.py:18
  260.7 20.0 %fusion.5 = bf16[5376,2048]{0,1:T(8,128)(2,1)} fusion(bf16[512,5376]{0,1:T(8,128)(2,1)} %all-gather.2.cloned.1.call-done, bf16[512,512]{0,1:T(8,128)(2,1)S(1)} %get-tuple-element.17, bf16[512,512]{0,1:T(8,128)(2,1)S(1)} %get-tuple-element.16, bf16[512,1024]{0,1:T(8,128)(2,1)S(1)} %bitcast.82), kind=kOutput, calls=%fused_computation.10 | convolution fusion | flops 11291590656 | bytes 29622272 | tf_op jit(solution)/shard_map/dot_general | solution.py:28
  280.7 28.2 %copy.50 = bf16[5376,2048]{1,0:T(8,128)(2,1)} copy(bf16[5376,2048]{0,1:T(8,128)(2,1)} %fusion.5) | data formatting | bytes 44040192
  309.0 13.0 %fusion.40 = f32[512,5376]{0,1:T(8,128)} fusion(bf16[5376,1024]{1,0:T(8,128)(2,1)} %param.7, bf16[512,1024]{0,1:T(8,128)(2,1)S(1)} %bitcast.83), kind=kOutput, calls=%fused_computation.67 | convolution fusion | flops 5637144576 | bytes 23068672 | tf_op jit(solution)/shard_map/dot_general | solution.py:22
  321.9 9.3 %fusion.36 = f32[512,5376]{0,1:T(8,128)} fusion(bf16[5376,512]{1,0:T(8,128)(2,1)} %param.8, bf16[2,512,512]{1,2,0:T(8,128)(2,1)S(1)} %fusion.22), kind=kOutput, calls=%fused_computation.63 | convolution fusion | flops 2818572288 | bytes 17039360 | tf_op jit(solution)/shard_map/dot_general | solution.py:22
  331.3 19.3 %add_convert_fusion = bf16[512,5376]{0,1:T(8,128)(2,1)} fusion(f32[512,5376]{0,1:T(8,128)} %fusion.40, f32[512,5376]{0,1:T(8,128)} %fusion.36, bf16[5376,512]{1,0:T(8,128)(2,1)} %param.9, bf16[2,512,512]{1,2,0:T(8,128)(2,1)S(1)} %fusion.22), kind=kOutput, calls=%fused_computation.17 | convolution fusion | flops 2826829824 | bytes 33554432 | tf_op jit(solution)/shard_map/dot_general | solution.py:22
  350.6 111.0 %reduce-scatter.7.cloned.1.call-done = bf16[672,2048]{1,0:T(8,128)(2,1)} async-done(((bf16[5376,2048]{1,0:T(8,128)(2,1)}), bf16[672,2048]{1,0:T(8,128)(2,1)}) %reduce-scatter.7.cloned.1.call-update) | async-done | bytes 2752528
  461.6 4.6 copy.51
  469.9 2.9 copy.33
  478.6 83.9 %reduce-scatter.5.cloned.1.call-done = bf16[512,1344]{0,1:T(8,128)(2,1)} async-done(((bf16[512,5376]{0,1:T(8,128)(2,1)}), bf16[512,1344]{0,1:T(8,128)(2,1)}) %reduce-scatter.5.cloned.1.call-update) | async-done | bytes 1376272 | tf_op jit(solution)/shard_map/reduce_scatter | solution.py:128
  (49 shorter events, 25.5 us)
Async XLA Ops:
  7.2 107.5 %all-gather.2.cloned.1.call-start = ((), (), s32[]{:S(2)}) async-start(), calls=%async_computation.2 | async-start | bytes 6881280 | tf_op jit(solution)/shard_map/all_gather | solution.py:88
  7.9 453.7 %reduce-scatter.7.cloned.1.call-start = ((), (), s32[]{:S(2)}) async-start(), calls=%async_computation.4 | async-start | bytes 24772608
  114.7 7.4 %copy-start.8 = (bf16[512,5376]{0,1:T(8,128)(2,1)S(1)}, bf16[512,5376]{0,1:T(8,128)(2,1)}, u32[]{:S(2)}) copy-start(bf16[512,5376]{0,1:T(8,128)(2,1)} %all-gather.2.cloned.1.call-done) | copy-start | bytes 16515076
  122.1 8.7 %copy-start.4 = (bf16[512,1024]{1,0:T(8,128)(2,1)S(1)}, bf16[512,1024]{1,0:T(8,128)(2,1)}, u32[]{:S(2)}) copy-start(bf16[512,1024]{1,0:T(8,128)(2,1)} %param.10) | copy-start | bytes 3145732
  122.1 10.0 %copy-start.7 = (s32[4096]{0:T(1024)S(1)}, s32[4096]{0:T(1024)}, u32[]{:S(2)}) copy-start(s32[4096]{0:T(1024)} %param.11) | copy-start | bytes 49156
  127.9 7.0 %collective-permute-start = (bf16[2,512,512]{2,1,0:T(8,128)(2,1)S(1)}, bf16[2,512,512]{2,1,0:T(8,128)(2,1)}, u32[]{:S(2)}, u32[]{:S(2)}) collective-permute-start(bf16[2,512,512]{2,1,0:T(8,128)(2,1)S(1)} %pad_maximum_fusion.1), channel_id=1, source_target_pairs={{0,4},{4,8},{8,12},{12,16},{16,20},{20,24},{24,28},{1,5},{5,9},{9,... | collective-permute-start | bytes 3145736 | tf_op jit(solution)/shard_map/ppermute | solution.py:18
  134.9 22.0 %collective-permute-start.1 = (bf16[2,512,512]{2,1,0:T(8,128)(2,1)}, bf16[2,512,512]{2,1,0:T(8,128)(2,1)S(1)}, u32[]{:S(2)}, u32[]{:S(2)}) collective-permute-start(bf16[2,512,512]{2,1,0:T(8,128)(2,1)} %collective-permute-done), channel_id=1, source_target_pairs={{0,4},{4,8},{8,12},{12,16},{16,20},{20,24},{24,28},{1,5},{5,9},{9,... | collective-permute-start | bytes 3145736 | tf_op jit(solution)/shard_map/ppermute | solution.py:18
  161.1 20.2 %copy-start.2 = (bf16[1536,4,128,1]{0,2,3,1:T(8,128)(2,1)}, bf16[1536,4,128,1]{0,2,3,1:T(8,128)(2,1)S(1)}, u32[]{:S(2)}) copy-start(bf16[1536,4,128,1]{0,2,3,1:T(8,128)(2,1)S(1)} %copy.38) | copy-start | bytes 4718596
  181.3 12.5 %copy-start.5 = (bf16[512,1024]{0,1:T(8,128)(2,1)S(1)}, bf16[512,1024]{0,1:T(8,128)(2,1)}, u32[]{:S(2)}) copy-start(bf16[512,1024]{0,1:T(8,128)(2,1)} %copy.53) | copy-start | bytes 3145732
  234.2 8.9 %copy-start = (f32[4,128,1536]{2,1,0:T(8,128)S(1)}, f32[4,128,1536]{2,1,0:T(8,128)}, u32[]{:S(2)}) copy-start(f32[4,128,1536]{2,1,0:T(8,128)} %fusion.13) | copy-start | bytes 9437188
  234.2 8.9 %copy-start.1 = (f32[4,1536,128,1]{1,2,3,0:T(8,128)S(1)}, f32[4,1536,128,1]{1,2,3,0:T(8,128)}, u32[]{:S(2)}) copy-start(f32[4,1536,128,1]{1,2,3,0:T(8,128)} %fusion.6) | copy-start | bytes 9437188
  236.1 8.7 %copy-start.3 = (bf16[1536,4,128,1]{0,2,3,1:T(8,128)(2,1)S(1)}, bf16[1536,4,128,1]{0,2,3,1:T(8,128)(2,1)}, u32[]{:S(2)}) copy-start(bf16[1536,4,128,1]{0,2,3,1:T(8,128)(2,1)} %copy-done.2) | copy-start | bytes 4718596
  236.1 7.0 %collective-permute-start.2 = (bf16[2,512,512]{1,2,0:T(8,128)(2,1)S(1)}, bf16[2,512,512]{1,2,0:T(8,128)(2,1)S(1)}, u32[]{:S(2)}, u32[]{:S(2)}) collective-permute-start(bf16[2,512,512]{1,2,0:T(8,128)(2,1)S(1)} %fusion.23), channel_id=1, source_target_pairs={{4,0},{8,4},{12,8},{16,12},{20,16},{24,20},{28,24},{5,1},{9,5},{13... | collective-permute-start | bytes 3145736 | tf_op jit(solution)/shard_map/ppermute | solution.py:18
  243.5 16.8 %collective-permute-start.3 = (bf16[2,512,512]{1,2,0:T(8,128)(2,1)S(1)}, bf16[2,512,512]{1,2,0:T(8,128)(2,1)S(1)}, u32[]{:S(2)}, u32[]{:S(2)}) collective-permute-start(bf16[2,512,512]{1,2,0:T(8,128)(2,1)S(1)} %fusion.19), channel_id=1, source_target_pairs={{4,0},{8,4},{12,8},{16,12},{20,16},{24,20},{28,24},{5,1},{9,5},{13... | collective-permute-start | bytes 3145736 | tf_op jit(solution)/shard_map/ppermute | solution.py:18
  247.6 13.1 %copy-start.6 = (bf16[4,128,2,512]{3,1,2,0:T(8,128)(2,1)S(1)}, bf16[4,128,2,512]{3,1,2,0:T(8,128)(2,1)}, u32[]{:S(2)}) copy-start(bf16[4,128,2,512]{3,1,2,0:T(8,128)(2,1)} %multiply_convert_fusion.1) | copy-start | bytes 3145732
  308.9 253.6 %reduce-scatter.5.cloned.1.call-start = ((), (), s32[]{:S(2)}) async-start(), calls=%async_computation.3 | async-start | bytes 6881280 | tf_op jit(solution)/shard_map/reduce_scatter | solution.py:128
Sparse Core Ops, SparseCore 0:
  9.6 105.0 all-gather.1
  309.0 152.5 reduce-scatter.6
  464.5 97.9 reduce-scatter.4
where the time goes:
time: 570 us; the launch traced here: 569 us
  waiting for transfers between devices  320 us (56%)
  matrix products  141 us (25%)
  local copies, waits for them, and re-layouts  51.1 us (9%)
  other arithmetic  26 us (5%)
  starting transfers between devices  16.2 us (3%)
  between operations  14 us (2%)
    unnamed x4, waiting for transfers between devices  112 us
    all_gather x1, waiting for transfers between devices, per_device(): gathered = lax.all_gather(tokens, 'head', axis=1, tiled=True)  107 us
    reduce_scatter x1, waiting for transfers between devices, per_device(): lax.psum_scatter(partial_term.astype(jnp.bfloat16), 'head', scatter_dimen...  83.9 us
    dot_general x3, matrix products, contract_last(): lax.dot_general(left, right, (((1,), (1,)), ((), ())), preferred_element_...  41.6 us
    unnamed x23, local copies, waits for them, and re-layouts  40.2 us
    dot_general x1, matrix products, contract_first(): lax.dot_general(left, right, (((0,), (0,)), ((), ())), preferred_element_...  20 us
    ppermute x4, waiting for transfers between devices, passed_along(): return lax.ppermute(x, axis, pairs)  18.1 us
    sub x1, matrix products, attend(): expo = jnp.where(allowed, jnp.exp(masked - row_max), 0.0)  17.4 us
  transfers between devices with their start and end apart: 7, of which 5 were waited for; matrix products, arithmetic and copies ran while one was open for 14% of the time, Pallas kernels for 0%

commit v1 on v0

--- a/solution.py
+++ b/solution.py
@@ -10,6 +10,19 @@
 WINDOW = 1024
 HOPS = 2
 neg_large = -1e30
+
+
+def gather_around(value, axis, dim):
+    ways = lax.axis_size(axis)
+    up = [(d, (d + 1) % ways) for d in range(ways)]
+    down = [(d, (d - 1) % ways) for d in range(ways)]
+    earlier, later = ([value], [value])
+    for _ in range(ways // 2):
+        earlier.append(lax.ppermute(earlier[-1], axis, up))
+    for _ in range((ways - 1) // 2):
+        later.append(lax.ppermute(later[-1], axis, down))
+    line = jnp.concatenate([*earlier[::-1], *later[1:]], axis=dim)
+    return jnp.roll(line, (lax.axis_index(axis) - ways // 2) * value.shape[dim], axis=dim)
 
 
 def passed_along(x, axis, by):
@@ -85,7 +98,7 @@
     tok_rows = tokens.shape[0]
     hop_count = HOPS
     margin = hop_count * tok_rows
-    gathered = lax.all_gather(tokens, "head", axis=1, tiled=True)
+    gathered = gather_around(tokens, "head", 1)
     queries = jnp.dot(gathered, query_weight, preferred_element_type=jnp.float32).astype(
         jnp.bfloat16
     )

time: 570 us -> 538 us (0.944)
  local copies, waits for them, and re-layouts: 51.1 us -> 18.6 us
  starting transfers between devices: 16.2 us -> 23.1 us
  waiting for transfers between devices: 320 us -> 314 us
    reduce_scatter x0 -> x1, waiting for transfers between devices: none -> 112 us  [per_device(): lax.psum_scatter(contract_first(gathered, proj_grads).astype(jnp.bfloat16...]
    unnamed x4 -> x2, waiting for transfers between devices: 112 us -> 0.03 us
    all_gather x1 -> x0, waiting for transfers between devices: 107 us -> none  [per_device(): gathered = lax.all_gather(tokens, 'head', axis=1, tiled=True)]
    ppermute x0 -> x3, waiting for transfers between devices: none -> 88.1 us  [the longest x2 63.6 us: gather_around(): earlier.append(lax.ppermute(earlier[-1], axis, up))]
    unnamed x23 -> x35, local copies, waits for them, and re-layouts: 40.2 us -> 6.24 us
    reduce_scatter x1, waiting for transfers between devices: 83.9 us -> 96.1 us  [per_device(): lax.psum_scatter(partial_term.astype(jnp.bfloat16), 'head', scatter_dimen...]
    ppermute x0 -> x3, starting transfers between devices: none -> 6.9 us  [the longest x1 3.82 us: gather_around(): later.append(lax.ppermute(later[-1], axis, down))]
  transfers between devices with their start and end apart: 7 -> 9, of which waited for: 5 -> 7; matrix products, arithmetic and copies ran while one was open for 14% -> 13% of each run, Pallas kernels for 0% -> 0%
where the time goes in v1:
time: 538 us; the launch traced here: 532 us
  waiting for transfers between devices  314 us (58%)
  matrix products  136 us (25%)
  other arithmetic  25.9 us (5%)
  starting transfers between devices  23.1 us (4%)
  local copies, waits for them, and re-layouts  18.6 us (3%)
  between operations  14.6 us (3%)
    reduce_scatter x1, waiting for transfers between devices, per_device(): lax.psum_scatter(contract_first(gathered, proj_grads).astype(jnp.bfloat16...  112 us
    reduce_scatter x1, waiting for transfers between devices, per_device(): lax.psum_scatter(partial_term.astype(jnp.bfloat16), 'head', scatter_dimen...  96.1 us
    ppermute x2, waiting for transfers between devices, gather_around(): earlier.append(lax.ppermute(earlier[-1], axis, up))  63.6 us
    dot_general x3, matrix products, contract_last(): lax.dot_general(left, right, (((1,), (1,)), ((), ())), preferred_element_...  41.8 us
    ppermute x1, waiting for transfers between devices, gather_around(): later.append(lax.ppermute(later[-1], axis, down))  24.5 us
    dot_general x1, matrix products, contract_first(): lax.dot_general(left, right, (((0,), (0,)), ((), ())), preferred_element_...  20.3 us
    sub x1, matrix products, attend(): expo = jnp.where(allowed, jnp.exp(masked - row_max), 0.0)  17.5 us
    ppermute x4, waiting for transfers between devices, passed_along(): return lax.ppermute(x, axis, pairs)  17.3 us
  transfers between devices with their start and end apart: 9, of which 7 were waited for; matrix products, arithmetic and copies ran while one was open for 13% of the time, Pallas kernels for 0%

profile of v1, /device:TPU:0, one launch (start us, length us, event | category | flops | bytes accessed | tf_op | source)
XLA Modules:
  0.0 531.8 jit_solution(1486726317921719031)
XLA Ops:
  7.2 3.1 collective-permute-start
  10.3 32.4 %collective-permute-done = bf16[512,1344]{0,1:T(8,128)(2,1)S(1)} collective-permute-done((bf16[512,1344]{0,1:T(8,128)(2,1)}, bf16[512,1344]{0,1:T(8,128)(2,1)S(1)}, u32[]{:S(2)}, u32[]{:S(2)}) %collective-permute-start) | collective-permute-done | bytes 1376288 | tf_op jit(solution)/shard_map/ppermute | solution.py:21
  42.7 3.8 collective-permute-start.2
  46.5 31.2 %collective-permute-done.1 = bf16[512,1344]{0,1:T(8,128)(2,1)} collective-permute-done((bf16[512,1344]{0,1:T(8,128)(2,1)S(1)}, bf16[512,1344]{0,1:T(8,128)(2,1)}, u32[]{:S(2)}, u32[]{:S(2)}) %collective-permute-start.1) | collective-permute-done | bytes 1376288 | tf_op jit(solution)/shard_map/ppermute | solution.py:21
  79.4 24.5 %collective-permute-done.2 = bf16[512,1344]{0,1:T(8,128)(2,1)} collective-permute-done((bf16[512,1344]{0,1:T(8,128)(2,1)}, bf16[512,1344]{0,1:T(8,128)(2,1)}, u32[]{:S(2)}, u32[]{:S(2)}) %collective-permute-start.2) | collective-permute-done | bytes 1376288 | tf_op jit(solution)/shard_map/ppermute | solution.py:23
  108.9 3.0 fusion.46
  113.2 3.0 fusion.49
  122.8 11.0 %collective-permute-start.4 = (bf16[2,512,512]{2,1,0:T(8,128)(2,1)}, bf16[2,512,512]{2,1,0:T(8,128)(2,1)S(1)}, u32[]{:S(2)}, u32[]{:S(2)}) collective-permute-start(bf16[2,512,512]{2,1,0:T(8,128)(2,1)} %collective-permute-done.3), channel_id=1, source_target_pairs={{0,4},{4,8},{8,12},{12,16},{16,20},{20,24},{24,28},{1,5},{5,9},{9,... | collective-permute-start | bytes 3145736 | tf_op jit(solution)/shard_map/ppermute | solution.py:31
  133.8 11.1 %fusion.37 = bf16[512,1024]{1,0:T(8,128)(2,1)S(1)} fusion(bf16[5376,1024]{1,0:T(8,128)(2,1)} %param.7, bf16[512,10752]{0,1:T(8,128)(2,1)} %copy-done.8, s32[]{:T(128)S(6)} %select_n.27), kind=kOutput, calls=%fused_computation.54 | convolution fusion | flops 5637668864 | bytes 17563652 | tf_op jit(solution)/shard_map/dot_general | solution.py:102
  150.4 2.8 reshape_squeeze.7
  153.1 17.5 %fusion.62 = (f32[4,2,512]{2,1,0:T(2,128)S(1)}, f32[4,2,512,1536]{2,3,1,0:T(8,128)}) fusion(pred[512,1536]{0,1:T(8,128)(4,1)} %fusion.22, bf16[1536,4,128,1]{0,2,3,1:T(8,128)(2,1)S(1)} %copy.22, bf16[512,4,2,128]{0,3,2,1:T(8,128)(2,1)} %bitcast.74), kind=kOutput, calls=%fused_computation.84 | convolution fusion | flops 1642071552 | bytes 28590080 | tf_op jit(solution)/shard_map/sub | solution.py:71
  170.7 12.6 %fusion.5 = f32[4,1536,128,1]{1,2,3,0:T(8,128)} fusion(bf16[512,4,2,128]{0,3,2,1:T(8,128)(2,1)} %bitcast.77, f32[4,2,512,1536]{2,3,1,0:T(8,128)} %get-tuple-element.11, f32[4,2,512]{2,1,0:T(2,128)S(1)} %get-tuple-element.10), kind=kOutput, calls=%fused_computation.10 | convolution fusion | flops 1623195648 | bytes 29376512 | tf_op jit(solution)/shard_map/kgac,akgd->ckd/dot_general | solution.py:91
  183.3 16.6 %fusion.1 = (f32[4,2,512]{2,1,0:T(2,128)S(1)}, f32[4,1536,512,2]{2,1,3,0:T(8,128)}) fusion(f32[4,2,512,1536]{2,3,1,0:T(8,128)} %get-tuple-element.11, f32[4,2,512]{2,1,0:T(2,128)S(1)} %get-tuple-element.10, bf16[512,4,2,128]{0,3,2,1:T(8,128)(2,1)S(1)} %bitcast.78, bf16[1536,4,128,1]{2,1,0,3:T(4,128)(2,1)S(1)} %bitcast.76), kind=kOutput, calls=%fused_computation.3 | convolution fusion | flops 1629483008 | bytes 52985856 | tf_op jit(solution)/shard_map/akgd,ckd->kgac/dot_general | solution.py:73
  199.9 16.8 %fusion.3 = bf16[4,2,512,1536]{2,3,1,0:T(8,128)(2,1)S(1)} fusion(f32[4,1536,512,2]{2,1,3,0:T(8,128)} %get-tuple-element.13, f32[4,2,512]{2,1,0:T(2,128)S(1)} %get-tuple-element.12, f32[4,2,512,1536]{2,3,1,0:T(8,128)} %get-tuple-element.11, f32[4,2,512]{2,1,0:T(2,128)S(1)} %get-tuple-element.10), kind=kLoop, calls=%fused_computation.5 | loop fusion | flops 25165824 | bytes 62947328 | tf_op jit(solution)/shard_map/convert_element_type | solution.py:77
  216.7 7.0 %fusion.19 = f32[4,128,1536]{2,1,0:T(8,128)} fusion(bf16[512,4,2,128]{0,3,2,1:T(8,128)(2,1)} %bitcast.75, bf16[4,2,512,1536]{2,3,1,0:T(8,128)(2,1)S(1)} %fusion.3), kind=kOutput, calls=%fused_computation.33 | convolution fusion | flops 1611399168 | bytes 16777216 | tf_op jit(solution)/shard_map/kgac,akgd->ckd/dot_general | solution.py:88
  227.2 5.3 collective-permute-done.5
  234.1 2.8 multiply_convert_fusion.1
  236.9 12.0 %collective-permute-done.6 = bf16[2,512,512]{1,2,0:T(8,128)(2,1)S(1)} collective-permute-done((bf16[2,512,512]{1,2,0:T(8,128)(2,1)S(1)}, bf16[2,512,512]{1,2,0:T(8,128)(2,1)S(1)}, u32[]{:S(2)}, u32[]{:S(2)}) %collective-permute-start.6) | collective-permute-done | bytes 1048608 | tf_op jit(solution)/shard_map/ppermute | solution.py:31
  249.4 20.3 %convolution_convert_fusion = bf16[5376,2048]{1,0:T(8,128)(2,1)} fusion(bf16[512,10752]{0,1:T(8,128)(2,1)} %copy-done.8, s32[]{:T(128)S(6)} %select_n.27, bf16[512,512]{0,1:T(8,128)(2,1)S(1)} %get-tuple-element.9, bf16[512,512]{0,1:T(8,128)(2,1)S(1)} %get-tuple-element.8, bf16[512,1024]{0,1:T(8,128)(2,1)S(1)} %bitcast.79), kind=kOutput, calls=%fused_computation.8 | convolution fusion | flops 11291590656 | bytes 29622276 | tf_op jit(solution)/shard_map/dot_general | solution.py:41
  269.8 12.9 %fusion.63 = f32[512,5376]{0,1:T(8,128)} fusion(bf16[5376,1024]{1,0:T(8,128)(2,1)} %param.7, bf16[512,1024]{0,1:T(8,128)(2,1)S(1)} %bitcast.80), kind=kOutput, calls=%fused_computation.85 | convolution fusion | flops 5637144576 | bytes 23068672 | tf_op jit(solution)/shard_map/dot_general | solution.py:35
  282.7 9.4 %fusion.59 = f32[512,5376]{0,1:T(8,128)} fusion(bf16[5376,512]{1,0:T(8,128)(2,1)} %param.8, bf16[2,512,512]{1,2,0:T(8,128)(2,1)S(1)} %fusion.28), kind=kOutput, calls=%fused_computation.81 | convolution fusion | flops 2818572288 | bytes 17039360 | tf_op jit(solution)/shard_map/dot_general | solution.py:35
  292.1 19.4 %add_convert_fusion = bf16[512,5376]{0,1:T(8,128)(2,1)} fusion(f32[512,5376]{0,1:T(8,128)} %fusion.63, f32[512,5376]{0,1:T(8,128)} %fusion.59, bf16[5376,512]{1,0:T(8,128)(2,1)} %param.9, bf16[2,512,512]{1,2,0:T(8,128)(2,1)S(1)} %fusion.28), kind=kOutput, calls=%fused_computation.16 | convolution fusion | flops 2826829824 | bytes 33554432 | tf_op jit(solution)/shard_map/dot_general | solution.py:35
  311.6 112.3 %reduce-scatter.5.cloned.1.call-done = bf16[672,2048]{1,0:T(8,128)(2,1)} async-done(((bf16[5376,2048]{1,0:T(8,128)(2,1)}), bf16[672,2048]{1,0:T(8,128)(2,1)}) %reduce-scatter.5.cloned.1.call-update) | async-done | bytes 2752528 | tf_op jit(solution)/shard_map/reduce_scatter | solution.py:145
  428.7 96.1 %reduce-scatter.3.cloned.1.call-done = bf16[512,1344]{0,1:T(8,128)(2,1)} async-done(((bf16[512,5376]{0,1:T(8,128)(2,1)}), bf16[512,1344]{0,1:T(8,128)(2,1)}) %reduce-scatter.3.cloned.1.call-update) | async-done | bytes 1376272 | tf_op jit(solution)/shard_map/reduce_scatter | solution.py:141
  (67 shorter events, 30.2 us)
Async XLA Ops:
  7.2 72.1 %copy-start.4 = (bf16[512,1344]{0,1:T(8,128)(2,1)S(1)}, bf16[512,1344]{0,1:T(8,128)(2,1)}, u32[]{:S(2)}) copy-start(bf16[512,1344]{0,1:T(8,128)(2,1)} %param.6) | copy-start | bytes 4128772
  7.2 416.7 %reduce-scatter.5.cloned.1.call-start = ((), (), s32[]{:S(2)}) async-start(), calls=%async_computation.3 | async-start | bytes 24772608 | tf_op jit(solution)/shard_map/reduce_scatter | solution.py:145
  7.2 35.5 %collective-permute-start = (bf16[512,1344]{0,1:T(8,128)(2,1)}, bf16[512,1344]{0,1:T(8,128)(2,1)S(1)}, u32[]{:S(2)}, u32[]{:S(2)}) collective-permute-start(bf16[512,1344]{0,1:T(8,128)(2,1)} %param.6), channel_id=1, source_target_pairs={{0,1},{1,2},{2,3},{3,0},{4,5},{5,6},{6,7},{7,4},{8,9},{9,10},{10,1... | collective-permute-start | bytes 4128776 | tf_op jit(solution)/shard_map/ppermute | solution.py:21
  42.7 35.0 %collective-permute-start.1 = (bf16[512,1344]{0,1:T(8,128)(2,1)S(1)}, bf16[512,1344]{0,1:T(8,128)(2,1)}, u32[]{:S(2)}, u32[]{:S(2)}) collective-permute-start(bf16[512,1344]{0,1:T(8,128)(2,1)S(1)} %collective-permute-done), channel_id=1, source_target_pairs={{0,1},{1,2},{2,3},{3,0},{4,5},{5,6},{6,7},{7,4},{8,9},{9,10},{10,1... | collective-permute-start | bytes 4128776 | tf_op jit(solution)/shard_map/ppermute | solution.py:21
  42.7 61.2 %collective-permute-start.2 = (bf16[512,1344]{0,1:T(8,128)(2,1)}, bf16[512,1344]{0,1:T(8,128)(2,1)}, u32[]{:S(2)}, u32[]{:S(2)}) collective-permute-start(bf16[512,1344]{0,1:T(8,128)(2,1)} %param.6), channel_id=1, source_target_pairs={{0,3},{1,0},{2,1},{3,2},{4,7},{5,4},{6,5},{7,6},{8,11},{9,8},{10,9... | collective-permute-start | bytes 4128776 | tf_op jit(solution)/shard_map/ppermute | solution.py:23
  103.9 4.9 slice-start
  107.0 1.8 slice-start.1
  107.2 6.0 %slice-start.2 = ((s8[5505024]{0:T(1024)(128)(4,1)}), s8[4194304]{0:T(1024)(128)(4,1)S(1)}, s32[]{:S(2)}) async-start(s8[5505024]{0:T(1024)(128)(4,1)} %bitcast.71), calls=%async_computation.6 | async-start | bytes 8388608
  108.8 4.4 copy-start.8
  108.8 4.3 slice-start.3
  113.2 5.5 %copy-start.5 = (bf16[512,1024]{1,0:T(8,128)(2,1)S(1)}, bf16[512,1024]{1,0:T(8,128)(2,1)}, u32[]{:S(2)}) copy-start(bf16[512,1024]{1,0:T(8,128)(2,1)} %param.10) | copy-start | bytes 3145732
  113.2 6.8 %copy-start.9 = (s32[4096]{0:T(1024)S(1)}, s32[4096]{0:T(1024)}, u32[]{:S(2)}) copy-start(s32[4096]{0:T(1024)} %param.11) | copy-start | bytes 49156
  116.4 6.4 %collective-permute-start.3 = (bf16[2,512,512]{2,1,0:T(8,128)(2,1)S(1)}, bf16[2,512,512]{2,1,0:T(8,128)(2,1)}, u32[]{:S(2)}, u32[]{:S(2)}) collective-permute-start(bf16[2,512,512]{2,1,0:T(8,128)(2,1)S(1)} %pad_maximum_fusion.1), channel_id=1, source_target_pairs={{0,4},{4,8},{8,12},{12,16},{16,20},{20,24},{24,28},{1,5},{5,9},{9,... | collective-permute-start | bytes 3145736 | tf_op jit(solution)/shard_map/ppermute | solution.py:31
  122.8 23.5 %collective-permute-start.4 = (bf16[2,512,512]{2,1,0:T(8,128)(2,1)}, bf16[2,512,512]{2,1,0:T(8,128)(2,1)S(1)}, u32[]{:S(2)}, u32[]{:S(2)}) collective-permute-start(bf16[2,512,512]{2,1,0:T(8,128)(2,1)} %collective-permute-done.3), channel_id=1, source_target_pairs={{0,4},{4,8},{8,12},{12,16},{16,20},{20,24},{24,28},{1,5},{5,9},{9,... | collective-permute-start | bytes 3145736 | tf_op jit(solution)/shard_map/ppermute | solution.py:31
  150.4 20.3 %copy-start.2 = (bf16[1536,4,128,1]{0,2,3,1:T(8,128)(2,1)}, bf16[1536,4,128,1]{0,2,3,1:T(8,128)(2,1)S(1)}, u32[]{:S(2)}) copy-start(bf16[1536,4,128,1]{0,2,3,1:T(8,128)(2,1)S(1)} %copy.22) | copy-start | bytes 4718596
  170.7 12.6 %copy-start.6 = (bf16[512,1024]{0,1:T(8,128)(2,1)S(1)}, bf16[512,1024]{0,1:T(8,128)(2,1)}, u32[]{:S(2)}) copy-start(bf16[512,1024]{0,1:T(8,128)(2,1)} %copy.35) | copy-start | bytes 3145732
  223.8 8.7 %copy-start = (f32[4,128,1536]{2,1,0:T(8,128)S(1)}, f32[4,128,1536]{2,1,0:T(8,128)}, u32[]{:S(2)}) copy-start(f32[4,128,1536]{2,1,0:T(8,128)} %fusion.19) | copy-start | bytes 9437188
  223.8 8.7 %copy-start.1 = (f32[4,1536,128,1]{1,2,3,0:T(8,128)S(1)}, f32[4,1536,128,1]{1,2,3,0:T(8,128)}, u32[]{:S(2)}) copy-start(f32[4,1536,128,1]{1,2,3,0:T(8,128)} %fusion.5) | copy-start | bytes 9437188
  225.6 8.5 %copy-start.3 = (bf16[1536,4,128,1]{0,2,3,1:T(8,128)(2,1)S(1)}, bf16[1536,4,128,1]{0,2,3,1:T(8,128)(2,1)}, u32[]{:S(2)}) copy-start(bf16[1536,4,128,1]{0,2,3,1:T(8,128)(2,1)} %copy-done.2) | copy-start | bytes 4718596
  225.6 6.8 %collective-permute-start.5 = (bf16[2,512,512]{1,2,0:T(8,128)(2,1)S(1)}, bf16[2,512,512]{1,2,0:T(8,128)(2,1)S(1)}, u32[]{:S(2)}, u32[]{:S(2)}) collective-permute-start(bf16[2,512,512]{1,2,0:T(8,128)(2,1)S(1)} %fusion.29), channel_id=1, source_target_pairs={{4,0},{8,4},{12,8},{16,12},{20,16},{24,20},{28,24},{5,1},{9,5},{13... | collective-permute-start | bytes 3145736 | tf_op jit(solution)/shard_map/ppermute | solution.py:31
  232.8 16.1 %collective-permute-start.6 = (bf16[2,512,512]{1,2,0:T(8,128)(2,1)S(1)}, bf16[2,512,512]{1,2,0:T(8,128)(2,1)S(1)}, u32[]{:S(2)}, u32[]{:S(2)}) collective-permute-start(bf16[2,512,512]{1,2,0:T(8,128)(2,1)S(1)} %fusion.25), channel_id=1, source_target_pairs={{4,0},{8,4},{12,8},{16,12},{20,16},{24,20},{28,24},{5,1},{9,5},{13... | collective-permute-start | bytes 3145736 | tf_op jit(solution)/shard_map/ppermute | solution.py:31
  236.9 12.5 %copy-start.7 = (bf16[4,128,2,512]{3,1,2,0:T(8,128)(2,1)S(1)}, bf16[4,128,2,512]{3,1,2,0:T(8,128)(2,1)}, u32[]{:S(2)}) copy-start(bf16[4,128,2,512]{3,1,2,0:T(8,128)(2,1)} %multiply_convert_fusion.1) | copy-start | bytes 3145732
  269.7 255.0 %reduce-scatter.3.cloned.1.call-start = ((), (), s32[]{:S(2)}) async-start(), calls=%async_computation.2 | async-start | bytes 6881280 | tf_op jit(solution)/shard_map/reduce_scatter | solution.py:141
Sparse Core Ops, SparseCore 0:
  269.8 153.9 reduce-scatter.4
  426.7 97.9 reduce-scatter.2
